TPU v7x, 512 devices: a whole 4x8x8 slice. The times are simulated.
512 devices in a mesh: dp: 64 (over x, z, y_lo), fsdp: 8 (over y_hi, core).
Axes of the slice: x: 4, y: 8 (y_hi: 4, y_lo: 2; y = y_hi * 2 + y_lo), z: 8, core: 2. Of those that a mesh axis runs over, the one named last changes fastest.
Arguments:
- group_qkv: bfloat16 [64, 1024, 6144], P('dp', 'fsdp'), may hold values from -6 to 6
- cache_pool: bfloat16 [8192, 16, 4096], P('dp', None, 'fsdp'), may hold values from -6 to 6
- page_request: int32 [8192], P('dp'), may hold values from 0 to 64, as said below
- request_host: int32 [64], replicated, may hold values from 0 to 63, each once
- out_weight: bfloat16 [2048, 2048], P(('dp', 'fsdp')), may hold values from -0.5 to 0.5
Outputs:
- projected: bfloat16 [64, 1024, 2048], P('dp', 'fsdp')
Inputs may be any that keep to these rules, and one draw needn't show every extreme that they name: `page_request`: within the slots of one dp index, at most 2 pages belong to one request, and some request has exactly 2 pages in the slots of every dp index. A request holds 1 to 15 pages, or 64 to 128 pages. Some slot is empty.
All inputs are finite; a program needn't handle non-finite values.
Results may differ from a plain program's by a relative error of at most 0.0053.
Values may be sent and summed in bfloat16 or wider, within the bound.
No kernel may reach another device: no remote copies, remote signals or barrier semaphores. Data moves between devices by JAX's collectives and lax.ppermute only.
A program may use at most 64 MiB of HBM per device.

v0:
```python
import math
import jax
import jax.numpy as jnp
from jax import lax
from jax.sharding import Mesh, PartitionSpec as P

HD = 128
PAGE = 16
MOST = 2
PHYSICAL_SPLIT = {"dp": (("x", 4), ("z", 8), ("y_lo", 2)), "fsdp": (("y_hi", 4), ("core", 2))}
DP = tuple((name for name, _ in PHYSICAL_SPLIT["dp"]))
FSDP = tuple((name for name, _ in PHYSICAL_SPLIT["fsdp"]))


def per_device(
    group_qkv, cache_pool, page_request, request_host, out_weight, *, fsdp_count, dp_count
):
    requests = request_host.shape[0]
    slot_count = page_request.shape[0]
    tokens_here = group_qkv.shape[1]
    features = cache_pool.shape[2]
    heads_here = features // (2 * HD)
    score_scale = 1.0 / math.sqrt(HD)
    width = out_weight.shape[1]
    weight = out_weight
    for name in reversed(DP[2:] + FSDP):
        weight = lax.all_gather(weight, name, axis=0, tiled=True)
    weight, group_qkv = lax.optimization_barrier((weight, group_qkv))
    weight = lax.all_gather(weight, DP[1], axis=0, tiled=True)
    local_qkv = group_qkv.reshape(tokens_here, fsdp_count, heads_here * 3 * HD)
    gathered_qkv = lax.all_to_all(local_qkv, FSDP, split_axis=1, concat_axis=0, tiled=True)
    group_len = tokens_here * fsdp_count
    gathered_qkv = gathered_qkv.reshape(group_len, heads_here, 3, HD)
    request_ids = jnp.arange(requests, dtype=jnp.int32)
    member = (page_request[:, None] == request_ids[None, :]).astype(jnp.int32)
    slot_rank = jnp.sum(member * (jnp.cumsum(member, axis=0) - 1), axis=1)
    target_host = jnp.sum(member * request_host[None, :], axis=1)
    is_live = jnp.sum(member, axis=1)
    target_slot = jnp.where(is_live > 0, target_host * MOST + slot_rank, -1)
    chosen = target_slot[:, None] == jnp.arange(requests * MOST, dtype=jnp.int32)[None, :]
    flat_pool = cache_pool.reshape(slot_count, PAGE * features)
    packed = jnp.einsum(
        "sp,sf->pf", chosen.astype(jnp.bfloat16), flat_pool, preferred_element_type=jnp.float32
    )
    occupied = jnp.sum(chosen.astype(jnp.int32), axis=0) > 0
    packed = jnp.where(occupied[:, None], packed, jnp.nan)
    packed = packed.astype(jnp.bfloat16).reshape(requests, MOST, PAGE, features)
    weight, packed = lax.optimization_barrier((weight, packed))
    weight = lax.all_gather(weight, DP[0], axis=0, tiled=True)
    arrived = lax.all_to_all(packed, DP, split_axis=0, concat_axis=0, tiled=True)
    present = jnp.logical_not(jnp.isnan(arrived[:, :, 0, 0]))
    live_tokens = jnp.repeat(present.reshape(requests * MOST), PAGE)
    cached = arrived.reshape(requests * MOST * PAGE, heads_here, 2, HD)
    key_cache = cached[:, :, 0]
    value_cache = jnp.where(
        live_tokens[:, None, None], cached[:, :, 1], jnp.zeros((), cached.dtype)
    )
    queries = gathered_qkv[:, :, 0]
    new_keys = gathered_qkv[:, :, 1]
    new_values = gathered_qkv[:, :, 2]
    block_rows = min(512, group_len)
    block_count = group_len // block_rows
    query_blocks = queries.reshape(block_count, block_rows, heads_here, HD)

    def attend(inputs):
        query_block, first_row = inputs
        cache_scores = (
            jnp.einsum("qhd,khd->hqk", query_block, key_cache, preferred_element_type=jnp.float32)
            * score_scale
        )
        cache_scores = jnp.where(live_tokens[None, None, :], cache_scores, -jnp.inf)
        group_scores = (
            jnp.einsum("qhd,khd->hqk", query_block, new_keys, preferred_element_type=jnp.float32)
            * score_scale
        )
        causal = jnp.arange(group_len)[None, :] <= first_row + jnp.arange(block_rows)[:, None]
        group_scores = jnp.where(causal[None, :, :], group_scores, -jnp.inf)
        row_max = jnp.maximum(jnp.max(cache_scores, axis=2), jnp.max(group_scores, axis=2))
        cache_expo = jnp.exp(cache_scores - row_max[:, :, None])
        group_expo = jnp.exp(group_scores - row_max[:, :, None])
        row_total = jnp.sum(cache_expo, axis=2) + jnp.sum(group_expo, axis=2)
        mixture = jnp.einsum(
            "hqk,khd->qhd",
            cache_expo.astype(jnp.bfloat16),
            value_cache,
            preferred_element_type=jnp.float32,
        )
        mixture = mixture + jnp.einsum(
            "hqk,khd->qhd",
            group_expo.astype(jnp.bfloat16),
            new_values,
            preferred_element_type=jnp.float32,
        )
        result = mixture / jnp.transpose(row_total)[:, :, None]
        return result.astype(jnp.bfloat16).reshape(block_rows, heads_here * HD)

    starts = jnp.arange(block_count, dtype=jnp.int32) * block_rows
    attn_heads = lax.map(attend, (query_blocks, starts)).reshape(group_len, heads_here * HD)
    tokens_attn = lax.all_to_all(attn_heads, FSDP, split_axis=0, concat_axis=1, tiled=True)
    summed = jnp.dot(tokens_attn, weight, preferred_element_type=jnp.float32)
    return summed.astype(jnp.bfloat16).reshape(1, tokens_here, width)


def solution(mesh):
    split = [part for axis in mesh.axis_names for part in PHYSICAL_SPLIT[axis]]
    fine = Mesh(mesh.devices.reshape([size for _, size in split]), DP + FSDP)
    return jax.shard_map(
        lambda *args: per_device(*args, fsdp_count=mesh.shape["fsdp"], dp_count=mesh.shape["dp"]),
        mesh=fine,
        in_specs=(P(DP, FSDP, None), P(DP, None, FSDP), P(DP), P(), P(DP + FSDP, None)),
        out_specs=P(DP, FSDP, None),
        check_vma=False,
    )
```

profile of v0, /device:TPU:64, one launch (start us, length us, event | category | flops | bytes accessed | tf_op | source)
XLA Modules:
  0.0 215.4 jit_solution(14413602714746578815)
XLA Ops:
  6.5 2.0 all-gather
  8.6 16.3 %all_gather.16 = bf16[32,2048]{1,0:T(8,128)(2,1)S(1)} all-gather(bf16[8,2048]{1,0:T(8,128)(2,1)S(1)} %reshape.84), channel_id=1, replica_groups=mesh['x'=4,'z'=8,'y_lo'=2,'y_hi'=4,'core'=2] {'y_hi'}, dimensions={0}, use_global_device_ids=true | all-gather | bytes 163840 | tf_op jit(solution)/shard_map/all_gather | solution.py:27
  24.9 5.7 %all_gather.17 = bf16[64,2048]{1,0:T(8,128)(2,1)} all-gather(bf16[32,2048]{1,0:T(8,128)(2,1)S(1)} %all_gather.16), channel_id=1, replica_groups=mesh['x'=4,'z'=8,'y_lo'=2,'y_hi'=4,'core'=2] {'y_lo'}, dimensions={0}, use_global_device_ids=true | all-gather | bytes 393216 | tf_op jit(solution)/shard_map/all_gather | solution.py:27
  30.6 2.6 %copy.38 = bf16[1,128,6144]{1,2,0:T(8,128)(2,1)} copy(bf16[1,128,6144]{2,1,0:T(8,128)(2,1)} %param.7) | data formatting | bytes 3145728 | tf_op jit(solution)/shard_map/optimization_barrier | solution.py:28
  33.2 4.9 %all-to-all-start.1 = ((bf16[128,8,768]{0,2,1:T(8,128)(2,1)}), bf16[128,8,768]{0,2,1:T(8,128)(2,1)}, u32[]{:S(2)}, u32[]{:S(2)}) async-start(bf16[128,8,768]{0,2,1:T(8,128)(2,1)} %bitcast.1), calls=%async_computation.1 | async-start | bytes 3145728 | tf_op jit(solution)/shard_map/all_to_all | solution.py:31
  38.1 3.0 %copy.51 = bf16[16,8,16,512]{3,1,2,0:T(8,128)(2,1)S(1)} copy(bf16[16,8,16,512]{3,2,1,0:T(8,128)(2,1)} %bitcast.86) | data formatting | bytes 4194304
  42.5 2.2 %copy.52 = bf16[16,8,16,512]{3,2,1,0:T(8,128)(2,1)} copy(bf16[16,8,16,512]{3,1,2,0:T(8,128)(2,1)S(1)} %bitcast.82) | data formatting | bytes 4194304
  44.7 31.3 %all-gather.4.cloned.1.call-done = bf16[512,2048]{1,0:T(8,128)(2,1)} async-done(((bf16[64,2048]{1,0:T(8,128)(2,1)}), bf16[512,2048]{1,0:T(8,128)(2,1)}) %all-gather.4.cloned.1.call-update) | async-done | bytes 2097168 | tf_op jit(solution)/shard_map/all_gather | solution.py:29
  76.0 2.5 %all-to-all-done.1 = bf16[128,8,768]{0,2,1:T(8,128)(2,1)} async-done(((bf16[128,8,768]{0,2,1:T(8,128)(2,1)}), bf16[128,8,768]{0,2,1:T(8,128)(2,1)}, u32[]{:S(2)}, u32[]{:S(2)}) %all-to-all-start.1) | async-done | bytes 1572896 | tf_op jit(solution)/shard_map/all_to_all | solution.py:31
  78.6 13.5 %all-to-all-start = ((bf16[64,2,16,512]{3,2,1,0:T(8,128)(2,1)}), bf16[64,2,16,512]{3,2,1,0:T(8,128)(2,1)S(1)}, u32[]{:S(2)}, u32[]{:S(2)}) async-start(bf16[64,2,16,512]{3,2,1,0:T(8,128)(2,1)} %bitcast.83), calls=%async_computation | async-start | bytes 4194304 | tf_op jit(solution)/shard_map/all_to_all | solution.py:50
  92.8 3.6 %copy.39 = bf16[8,128,1,768]{1,0,3,2:T(8,128)(2,1)} copy(bf16[8,128,1,768]{1,3,0,2:T(8,128)(2,1)} %bitcast.3) | data formatting | bytes 3145728 | tf_op jit(solution)/shard_map/all_to_all | solution.py:31
  96.5 3.7 %reshape.80 = bf16[1024,2,3,128]{0,3,2,1:T(8,128)(2,1)} reshape(bf16[8,128,1,768]{1,0,3,2:T(8,128)(2,1)} %copy.39) | data formatting | bytes 3145728 | tf_op jit(solution)/shard_map/reshape | solution.py:33
  100.1 2.5 %slice_bitcast_fusion = (bf16[1024,2,128]{0,2,1:T(8,128)(2,1)}, bf16[1024,2,1,128]{0,3,2,1:T(8,128)(2,1)}, bf16[1024,2,1,128]{0,3,2,1:T(8,128)(2,1)S(1)}) fusion(bf16[1024,2,3,128]{0,3,2,1:T(8,128)(2,1)} %reshape.80), kind=kLoop, calls=%fused_computation.41 | loop fusion | bytes 3145728 | tf_op jit(solution)/shard_map/squeeze | solution.py:60
  102.9 1.3 copy.42
  104.3 37.4 %all-to-all-done = bf16[64,2,16,512]{3,2,1,0:T(8,128)(2,1)S(1)} async-done(((bf16[64,2,16,512]{3,2,1,0:T(8,128)(2,1)}), bf16[64,2,16,512]{3,2,1,0:T(8,128)(2,1)S(1)}, u32[]{:S(2)}, u32[]{:S(2)}) %all-to-all-start) | async-done | bytes 2097184 | tf_op jit(solution)/shard_map/all_to_all | solution.py:50
  141.7 2.4 %not_reduce_fusion = pred[64,2]{1,0:T(8,128)(4,1)S(1)} fusion(bf16[64,2,16,512]{3,2,1,0:T(8,128)(2,1)S(1)} %all-to-all-done), kind=kLoop, calls=%fused_computation.42 | loop fusion | flops 384 | bytes 384 | tf_op jit(solution)/shard_map/not | solution.py:51
  144.4 2.6 %reshape.81 = bf16[2048,2,2,128]{3,2,1,0:T(2,128)(2,1)S(1)} reshape(bf16[64,2,16,512]{3,2,1,0:T(8,128)(2,1)} %copy-done.1) | data formatting | bytes 4194304 | tf_op jit(solution)/shard_map/reshape | solution.py:53
  147.0 3.9 %fusion.43 = (bf16[2048,2,1,128]{3,2,1,0:T(2,128)(2,1)S(1)}, bf16[2048,2,1,128]{3,2,1,0:T(2,128)(2,1)}) fusion(bf16[2048,2,2,128]{3,2,1,0:T(2,128)(2,1)S(1)} %reshape.81), kind=kLoop, calls=%fused_computation.54 | loop fusion | bytes 4194304 | tf_op jit(solution)/shard_map/slice | solution.py:56
  151.5 1.3 copy.45
  152.9 1.8 copy.55
  154.6 27.4 %while.11 = (s32[]{:T(128)}, bf16[2,512,256]{2,1,0:T(8,128)(2,1)S(1)}, bf16[2,512,2,128]{3,1,0,2:T(8,128)(2,1)S(1)}, bf16[2048,2,128]{2,0,1:T(8,128)(2,1)S(1)}, ...) while((s32[]{:T(128)}, ...), condition=%wide.region_10.11_spmd.clone, body=%wide.region_5.10_spmd.clone.sunk | while | flops 1646131712 | bytes 69022040 | solution.py:98
  156.3 2.9 %fusion.69 = (f32[2,512]{1,0:T(2,128)S(1)}, f32[2,512,1024]{2,1,0:T(8,128)}) fusion(pred[512,1024]{1,0:T(8,128)(4,1)S(1)} %iota_compare_fusion.5, bf16[1024,2,128]{2,0,1:T(8,128)(2,1)S(1)} %get-tuple-element.236, bf16[2,512,2,128]{3,1,0,2:T(8,128)(2,1)S(1)} %get-tuple-element.233, s32[]{:T(128)} %get-tuple-element.221), kind=kOutput, calls=%fused_computation.10.clone.1 | convolution fusion | flops 271580160 | bytes 5509124 | tf_op jit(solution)/shard_map/while/body/eval_jaxpr/qhd,khd->hqk/dot_general | solution.py:73
  159.3 1.4 fusion.70
  162.8 1.9 fusion.72
  164.7 1.3 fusion.71
  166.0 2.2 %fusion.74 = bf16[512,2,128]{0,2,1:T(8,128)(2,1)S(1)} fusion(f32[2,512,128]{1,2,0:T(8,128)S(1)} %fusion.71, bf16[2048,2,128]{0,2,1:T(8,128)(2,1)S(1)} %copy-done.2, f32[2,512,2048]{2,1,0:T(8,128)S(1)} %get-tuple-element.210, f32[2,512]{1,0:T(2,128)S(1)} %max.9, pred[2048]{0:T(1024)(128)(4,1)S(1)} %broadcast_in_dim.164, ...), kind=kOutput, calls=%fused_computation.19.clone.1 | convolution fusion | flops 545652736 | bytes 10233856 | tf_op jit(solution)/shard_map/while/body/eval_jaxpr/hqk,khd->qhd/dot_general | solution.py:82
  170.0 2.9 %fusion.69 = (f32[2,512]{1,0:T(2,128)S(1)}, f32[2,512,1024]{2,1,0:T(8,128)}) fusion(pred[512,1024]{1,0:T(8,128)(4,1)S(1)} %iota_compare_fusion.5, bf16[1024,2,128]{2,0,1:T(8,128)(2,1)S(1)} %get-tuple-element.236, bf16[2,512,2,128]{3,1,0,2:T(8,128)(2,1)S(1)} %get-tuple-element.233, s32[]{:T(128)} %get-tuple-element.221), kind=kOutput, calls=%fused_computation.10.clone.1 | convolution fusion | flops 271580160 | bytes 5509124 | tf_op jit(solution)/shard_map/while/body/eval_jaxpr/qhd,khd->hqk/dot_general | solution.py:73
  173.1 1.4 fusion.70
  176.5 1.9 fusion.72
  179.7 2.2 %fusion.74 = bf16[512,2,128]{0,2,1:T(8,128)(2,1)S(1)} fusion(f32[2,512,128]{1,2,0:T(8,128)S(1)} %fusion.71, bf16[2048,2,128]{0,2,1:T(8,128)(2,1)S(1)} %copy-done.2, f32[2,512,2048]{2,1,0:T(8,128)S(1)} %get-tuple-element.210, f32[2,512]{1,0:T(2,128)S(1)} %max.9, pred[2048]{0:T(1024)(128)(4,1)S(1)} %broadcast_in_dim.164, ...), kind=kOutput, calls=%fused_computation.19.clone.1 | convolution fusion | flops 545652736 | bytes 10233856 | tf_op jit(solution)/shard_map/while/body/eval_jaxpr/hqk,khd->qhd/dot_general | solution.py:82
  182.1 20.7 %all_to_all.39 = bf16[8,128,256]{2,1,0:T(8,128)(2,1)S(1)} all-to-all(bf16[8,128,256]{2,1,0:T(8,128)(2,1)S(1)} %bitcast.88), channel_id=1, replica_groups=mesh['x'=4,'z'=8,'y_lo'=2,'y_hi'=4,'core'=2] {'y_hi','core'}, dimensions={0} | all-to-all | bytes 1048576 | tf_op jit(solution)/shard_map/all_to_all | solution.py:99
  203.1 5.5 %fusion.39 = bf16[1,128,2048]{2,1,0:T(8,128)(2,1)} fusion(bf16[128,2048]{0,1:T(8,128)(2,1)S(1)} %bitcast.85, bf16[2048,2048]{1,0:T(8,128)(2,1)} %all-gather.6.cloned.1.call-done), kind=kOutput, calls=%fused_computation.38 | convolution fusion | flops 1074003968 | bytes 9437184 | tf_op jit(solution)/shard_map/dot_general | solution.py:100
  (62 shorter events, 12.9 us)
Async XLA Ops:
  6.5 69.5 %all-gather.4.cloned.1.call-start = ((), (), s32[]{:S(2)}) async-start(), calls=%async_computation.3 | async-start | bytes 2359296 | tf_op jit(solution)/shard_map/all_gather | solution.py:29
  33.2 7.9 %copy-start.5 = (s32[128]{0:T(128)S(1)}, s32[128]{0:T(128)}, u32[]{:S(2)}) copy-start(s32[128]{0:T(128)} %param.9) | copy-start | bytes 1540
  33.2 8.1 %copy-start.6 = (s32[64]{0:T(128)S(1)}, s32[64]{0:T(128)}, u32[]{:S(2)}) copy-start(s32[64]{0:T(128)} %param.10) | copy-start | bytes 772
  33.2 45.3 %all-to-all-start.1 = ((bf16[128,8,768]{0,2,1:T(8,128)(2,1)}), bf16[128,8,768]{0,2,1:T(8,128)(2,1)}, u32[]{:S(2)}, u32[]{:S(2)}) async-start(bf16[128,8,768]{0,2,1:T(8,128)(2,1)} %bitcast.1), calls=%async_computation.1 | async-start | bytes 3145728 | tf_op jit(solution)/shard_map/all_to_all | solution.py:31
  78.6 63.1 %all-to-all-start = ((bf16[64,2,16,512]{3,2,1,0:T(8,128)(2,1)}), bf16[64,2,16,512]{3,2,1,0:T(8,128)(2,1)S(1)}, u32[]{:S(2)}, u32[]{:S(2)}) async-start(bf16[64,2,16,512]{3,2,1,0:T(8,128)(2,1)} %bitcast.83), calls=%async_computation | async-start | bytes 4194304 | tf_op jit(solution)/shard_map/all_to_all | solution.py:50
  92.1 111.0 %all-gather.6.cloned.1.call-start = ((), (), s32[]{:S(2)}) async-start(), calls=%async_computation.4 | async-start | bytes 10485760 | tf_op jit(solution)/shard_map/all_gather | solution.py:49
  141.7 2.6 %copy-start.1 = (bf16[64,2,16,512]{3,2,1,0:T(8,128)(2,1)}, bf16[64,2,16,512]{3,2,1,0:T(8,128)(2,1)S(1)}, u32[]{:S(2)}) copy-start(bf16[64,2,16,512]{3,2,1,0:T(8,128)(2,1)S(1)} %all-to-all-done) | copy-start | bytes 6291460
  150.9 3.8 %copy-start.3 = (bf16[2,512,256]{2,1,0:T(8,128)(2,1)S(1)}, bf16[2,512,256]{2,1,0:T(8,128)(2,1)}, u32[]{:S(2)}) copy-start(bf16[2,512,256]{2,1,0:T(8,128)(2,1)} %custom-call) | copy-start | bytes 1572868
  159.3 2.3 %copy-start = (f32[2,512,1024]{2,1,0:T(8,128)S(1)}, f32[2,512,1024]{2,1,0:T(8,128)}, u32[]{:S(2)}) copy-start(f32[2,512,1024]{2,1,0:T(8,128)} %get-tuple-element.207) | copy-start | bytes 12582916 | tf_op jit(solution)/shard_map/while
  162.8 1.9 copy-start.4
  164.7 1.4 copy-start.2
  173.1 2.2 %copy-start = (f32[2,512,1024]{2,1,0:T(8,128)S(1)}, f32[2,512,1024]{2,1,0:T(8,128)}, u32[]{:S(2)}) copy-start(f32[2,512,1024]{2,1,0:T(8,128)} %get-tuple-element.207) | copy-start | bytes 12582916 | tf_op jit(solution)/shard_map/while
  176.5 1.9 copy-start.4
  178.3 1.4 copy-start.2
Sparse Core Ops, SparseCore 0:
  30.7 45.2 all-gather.3
  95.0 97.7 all-gather.5
where the time goes:
time: 216 us; the launch traced here: 215 us
  waiting for transfers between devices  72 us (33%)
  blocking collectives  44.8 us (21%)
  local copies, waits for them, and re-layouts  32.8 us (15%)
  matrix products  21.8 us (10%)
  starting transfers between devices  18.4 us (9%)
  between operations  13.5 us (6%)
  other arithmetic  11.8 us (5%)
    all_to_all x1, waiting for transfers between devices, per_device(): lax.all_to_all(packed, DP, split_axis=0, concat_axis=0, tiled=True)  37.4 us
    all_gather x1, waiting for transfers between devices, per_device(): weight = lax.all_gather(weight, DP[1], axis=0, tiled=True)  31.3 us
    all_gather x3, blocking collectives, per_device(): weight = lax.all_gather(weight, name, axis=0, tiled=True)  24 us
    all_to_all x1, blocking collectives, per_device(): lax.all_to_all(attn_heads, FSDP, split_axis=0, concat_axis=1, tiled=True)  20.7 us
    all_to_all x1, starting transfers between devices, per_device(): lax.all_to_all(packed, DP, split_axis=0, concat_axis=0, tiled=True)  13.5 us
    unnamed x12, local copies, waits for them, and re-layouts  6.55 us
    reduce_sum x4, other arithmetic, attend(): row_total = jnp.sum(cache_expo, axis=2) + jnp.sum(group_expo, axis=2)  6.12 us
    dot_general x2, matrix products, attend(): jnp.einsum('qhd,khd->hqk', query_block, new_keys, preferred_element_type=...  5.78 us
  transfers between devices with their start and end apart: 4, of which 3 were waited for; matrix products, arithmetic and copies ran while one was open for 28% of the time, Pallas kernels for 0%

commit v1 on v0

--- a/solution.py
+++ b/solution.py
@@ -10,6 +10,11 @@
 PHYSICAL_SPLIT = {"dp": (("x", 4), ("z", 8), ("y_lo", 2)), "fsdp": (("y_hi", 4), ("core", 2))}
 DP = tuple((name for name, _ in PHYSICAL_SPLIT["dp"]))
 FSDP = tuple((name for name, _ in PHYSICAL_SPLIT["fsdp"]))
+
+
+def all_by_exchange(value, axis, dim):
+    sent = jnp.stack([value] * lax.axis_size(axis))
+    return jnp.concatenate(lax.all_to_all(sent, axis, 0, 0), axis=dim)
 
 
 def per_device(
@@ -26,7 +31,7 @@
     for name in reversed(DP[2:] + FSDP):
         weight = lax.all_gather(weight, name, axis=0, tiled=True)
     weight, group_qkv = lax.optimization_barrier((weight, group_qkv))
-    weight = lax.all_gather(weight, DP[1], axis=0, tiled=True)
+    weight = all_by_exchange(weight, DP[1], 0)
     local_qkv = group_qkv.reshape(tokens_here, fsdp_count, heads_here * 3 * HD)
     gathered_qkv = lax.all_to_all(local_qkv, FSDP, split_axis=1, concat_axis=0, tiled=True)
     group_len = tokens_here * fsdp_count

time: 216 us -> 264 us (1.22)
  the two profiles are of different devices: /device:TPU:64 before, /device:TPU:1 now
where the time goes in v1:
time: 264 us; the launch traced here: 263 us
  waiting for transfers between devices  112 us (42%)
  blocking collectives  48.3 us (18%)
  local copies, waits for them, and re-layouts  34.4 us (13%)
  matrix products  21.8 us (8%)
  starting transfers between devices  21.2 us (8%)
  between operations  13.5 us (5%)
  other arithmetic  11.8 us (4%)
    all_to_all x1, waiting for transfers between devices, all_by_exchange(): return jnp.concatenate(lax.all_to_all(sent, axis, 0, 0), axis=dim)  45.2 us
    all_to_all x1, waiting for transfers between devices, per_device(): lax.all_to_all(packed, DP, split_axis=0, concat_axis=0, tiled=True)  35.3 us
    all_to_all x1, waiting for transfers between devices, per_device(): lax.all_to_all(local_qkv, FSDP, split_axis=1, concat_axis=0, tiled=True)  30.6 us
    all_to_all x1, blocking collectives, per_device(): lax.all_to_all(attn_heads, FSDP, split_axis=0, concat_axis=1, tiled=True)  24.4 us
    all_gather x3, blocking collectives, per_device(): weight = lax.all_gather(weight, name, axis=0, tiled=True)  23.9 us
    all_to_all x1, starting transfers between devices, per_device(): lax.all_to_all(local_qkv, FSDP, split_axis=1, concat_axis=0, tiled=True)  8.88 us
    all_to_all x1, starting transfers between devices, all_by_exchange(): return jnp.concatenate(lax.all_to_all(sent, axis, 0, 0), axis=dim)  7.28 us
    unnamed x14, local copies, waits for them, and re-layouts  6.56 us
  transfers between devices with their start and end apart: 4, of which 3 were waited for; matrix products, arithmetic and copies ran while one was open for 23% of the time, Pallas kernels for 0%

profile of v1, /device:TPU:1, one launch (start us, length us, event | category | flops | bytes accessed | tf_op | source)
XLA Modules:
  0.0 263.1 jit_solution(13853678462268318374)
XLA Ops:
  6.5 8.5 %all-gather = bf16[2,4,2048]{2,1,0:T(4,128)(2,1)S(1)} all-gather(bf16[1,4,2048]{2,1,0:T(4,128)(2,1)} %bitcast.92), channel_id=1, replica_groups=mesh['x'=4,'z'=8,'y_lo'=2,'y_hi'=4,'core'=2] {'core'}, dimensions={0}, use_global_device_ids=true | all-gather | bytes 49152 | tf_op jit(solution)/shard_map/all_gather | solution.py:32
  15.1 10.9 %all_gather.13 = bf16[32,2048]{1,0:T(8,128)(2,1)S(1)} all-gather(bf16[8,2048]{1,0:T(8,128)(2,1)S(1)} %reshape.90), channel_id=1, replica_groups=mesh['x'=4,'z'=8,'y_lo'=2,'y_hi'=4,'core'=2] {'y_hi'}, dimensions={0}, use_global_device_ids=true | all-gather | bytes 163840 | tf_op jit(solution)/shard_map/all_gather | solution.py:32
  26.0 4.5 %all_gather.14 = bf16[64,2048]{1,0:T(8,128)(2,1)S(1)} all-gather(bf16[32,2048]{1,0:T(8,128)(2,1)S(1)} %all_gather.13), channel_id=1, replica_groups=mesh['x'=4,'z'=8,'y_lo'=2,'y_hi'=4,'core'=2] {'y_lo'}, dimensions={0}, use_global_device_ids=true | all-gather | bytes 393216 | tf_op jit(solution)/shard_map/all_gather | solution.py:32
  30.4 1.6 stack.2
  32.1 7.3 %all-to-all-start = ((bf16[8,64,2048]{2,1,0:T(8,128)(2,1)}), bf16[8,64,2048]{2,1,0:T(8,128)(2,1)S(1)}, u32[]{:S(2)}, u32[]{:S(2)}) async-start(bf16[8,64,2048]{2,1,0:T(8,128)(2,1)} %stack.2), calls=%async_computation | async-start | bytes 4194304 | tf_op jit(solution)/shard_map/all_to_all | solution.py:17
  39.3 2.6 copy.38
  41.9 45.2 %all-to-all-done = bf16[8,64,2048]{2,1,0:T(8,128)(2,1)S(1)} async-done(((bf16[8,64,2048]{2,1,0:T(8,128)(2,1)}), bf16[8,64,2048]{2,1,0:T(8,128)(2,1)S(1)}, u32[]{:S(2)}, u32[]{:S(2)}) %all-to-all-start) | async-done | bytes 2097184 | tf_op jit(solution)/shard_map/all_to_all | solution.py:17
  87.1 8.9 %all-to-all-start.2 = ((bf16[128,8,768]{0,2,1:T(8,128)(2,1)}), bf16[128,8,768]{0,2,1:T(8,128)(2,1)}, u32[]{:S(2)}, u32[]{:S(2)}) async-start(bf16[128,8,768]{0,2,1:T(8,128)(2,1)} %bitcast.87), calls=%async_computation.2 | async-start | bytes 3145728 | tf_op jit(solution)/shard_map/all_to_all | solution.py:36
  96.0 3.0 %copy.51 = bf16[16,8,16,512]{3,1,2,0:T(8,128)(2,1)S(1)} copy(bf16[16,8,16,512]{3,2,1,0:T(8,128)(2,1)} %bitcast.89) | data formatting | bytes 4194304
  100.4 2.2 copy.52
  102.7 30.6 %all-to-all-done.2 = bf16[128,8,768]{0,2,1:T(8,128)(2,1)} async-done(((bf16[128,8,768]{0,2,1:T(8,128)(2,1)}), bf16[128,8,768]{0,2,1:T(8,128)(2,1)}, u32[]{:S(2)}, u32[]{:S(2)}) %all-to-all-start.2) | async-done | bytes 1572896 | tf_op jit(solution)/shard_map/all_to_all | solution.py:36
  133.3 5.0 %all-to-all-start.1 = ((bf16[64,2,16,512]{3,2,1,0:T(8,128)(2,1)}), bf16[64,2,16,512]{3,2,1,0:T(8,128)(2,1)S(1)}, u32[]{:S(2)}, u32[]{:S(2)}) async-start(bf16[64,2,16,512]{3,2,1,0:T(8,128)(2,1)} %bitcast.85), calls=%async_computation.1 | async-start | bytes 4194304 | tf_op jit(solution)/shard_map/all_to_all | solution.py:55
  139.1 3.6 %copy.39 = bf16[8,128,1,768]{1,0,3,2:T(8,128)(2,1)} copy(bf16[8,128,1,768]{1,3,0,2:T(8,128)(2,1)} %bitcast.3) | data formatting | bytes 3145728 | tf_op jit(solution)/shard_map/all_to_all | solution.py:36
  142.7 3.7 %reshape.86 = bf16[1024,2,3,128]{0,3,2,1:T(8,128)(2,1)} reshape(bf16[8,128,1,768]{1,0,3,2:T(8,128)(2,1)} %copy.39) | data formatting | bytes 3145728 | tf_op jit(solution)/shard_map/reshape | solution.py:38
  146.4 2.5 slice_bitcast_fusion
  150.5 35.3 %all-to-all-done.1 = bf16[64,2,16,512]{3,2,1,0:T(8,128)(2,1)S(1)} async-done(((bf16[64,2,16,512]{3,2,1,0:T(8,128)(2,1)}), bf16[64,2,16,512]{3,2,1,0:T(8,128)(2,1)S(1)}, u32[]{:S(2)}, u32[]{:S(2)}) %all-to-all-start.1) | async-done | bytes 2097184 | tf_op jit(solution)/shard_map/all_to_all | solution.py:55
  185.7 2.4 not_reduce_fusion
  188.5 2.6 reshape.87
  191.0 3.9 %fusion.43 = (bf16[2048,2,1,128]{3,2,1,0:T(2,128)(2,1)S(1)}, bf16[2048,2,1,128]{3,2,1,0:T(2,128)(2,1)}) fusion(bf16[2048,2,2,128]{3,2,1,0:T(2,128)(2,1)S(1)} %reshape.87), kind=kLoop, calls=%fused_computation.54 | loop fusion | bytes 4194304 | tf_op jit(solution)/shard_map/slice | solution.py:61
  195.6 1.3 copy.45
  196.9 1.8 copy.55
  198.7 27.4 %while.11 = (s32[]{:T(128)}, bf16[2,512,256]{2,1,0:T(8,128)(2,1)S(1)}, bf16[2,512,2,128]{3,1,0,2:T(8,128)(2,1)S(1)}, bf16[2048,2,128]{2,0,1:T(8,128)(2,1)S(1)}, ...) while((s32[]{:T(128)}, ...), condition=%wide.region_10.11_spmd.clone, body=%wide.region_5.10_spmd.clone.sunk | while | flops 1646131712 | bytes 69022040 | solution.py:103
  200.3 2.9 %fusion.69 = (f32[2,512]{1,0:T(2,128)S(1)}, f32[2,512,1024]{2,1,0:T(8,128)}) fusion(pred[512,1024]{1,0:T(8,128)(4,1)S(1)} %iota_compare_fusion.5, bf16[1024,2,128]{2,0,1:T(8,128)(2,1)S(1)} %get-tuple-element.236, bf16[2,512,2,128]{3,1,0,2:T(8,128)(2,1)S(1)} %get-tuple-element.233, s32[]{:T(128)} %get-tuple-element.221), kind=kOutput, calls=%fused_computation.10.clone.1 | convolution fusion | flops 271580160 | bytes 5509124 | tf_op jit(solution)/shard_map/while/body/eval_jaxpr/qhd,khd->hqk/dot_general | solution.py:78
  203.4 1.4 fusion.70
  206.9 1.9 fusion.72
  210.1 2.2 fusion.74
  214.1 2.9 %fusion.69 = (f32[2,512]{1,0:T(2,128)S(1)}, f32[2,512,1024]{2,1,0:T(8,128)}) fusion(pred[512,1024]{1,0:T(8,128)(4,1)S(1)} %iota_compare_fusion.5, bf16[1024,2,128]{2,0,1:T(8,128)(2,1)S(1)} %get-tuple-element.236, bf16[2,512,2,128]{3,1,0,2:T(8,128)(2,1)S(1)} %get-tuple-element.233, s32[]{:T(128)} %get-tuple-element.221), kind=kOutput, calls=%fused_computation.10.clone.1 | convolution fusion | flops 271580160 | bytes 5509124 | tf_op jit(solution)/shard_map/while/body/eval_jaxpr/qhd,khd->hqk/dot_general | solution.py:78
  217.1 1.4 fusion.70
  220.5 1.9 fusion.72
  223.8 2.2 fusion.74
  226.1 24.4 %all_to_all.44 = bf16[8,128,256]{2,1,0:T(8,128)(2,1)S(1)} all-to-all(bf16[8,128,256]{2,1,0:T(8,128)(2,1)S(1)} %bitcast.91), channel_id=1, replica_groups=mesh['x'=4,'z'=8,'y_lo'=2,'y_hi'=4,'core'=2] {'y_hi','core'}, dimensions={0} | all-to-all | bytes 1048576 | tf_op jit(solution)/shard_map/all_to_all | solution.py:104
  250.8 5.5 %fusion.39 = bf16[1,128,2048]{2,1,0:T(8,128)(2,1)} fusion(bf16[128,2048]{0,1:T(8,128)(2,1)S(1)} %bitcast.88, bf16[2048,2048]{1,0:T(8,128)(2,1)} %all-gather.3.cloned.1.call-done), kind=kOutput, calls=%fused_computation.38 | convolution fusion | flops 1074003968 | bytes 9437184 | tf_op jit(solution)/shard_map/dot_general | solution.py:105
  (64 shorter events, 15.5 us)
Async XLA Ops:
  32.1 55.1 %all-to-all-start = ((bf16[8,64,2048]{2,1,0:T(8,128)(2,1)}), bf16[8,64,2048]{2,1,0:T(8,128)(2,1)S(1)}, u32[]{:S(2)}, u32[]{:S(2)}) async-start(bf16[8,64,2048]{2,1,0:T(8,128)(2,1)} %stack.2), calls=%async_computation | async-start | bytes 4194304 | tf_op jit(solution)/shard_map/all_to_all | solution.py:17
  41.9 57.1 %copy-start.6 = (s32[128]{0:T(128)S(1)}, s32[128]{0:T(128)}, u32[]{:S(2)}) copy-start(s32[128]{0:T(128)} %param.9) | copy-start | bytes 1540
  41.9 57.4 %copy-start.7 = (s32[64]{0:T(128)S(1)}, s32[64]{0:T(128)}, u32[]{:S(2)}) copy-start(s32[64]{0:T(128)} %param.10) | copy-start | bytes 772
  87.1 8.9 %copy-start.2 = (bf16[8,64,2048]{2,1,0:T(8,128)(2,1)}, bf16[8,64,2048]{2,1,0:T(8,128)(2,1)S(1)}, u32[]{:S(2)}) copy-start(bf16[8,64,2048]{2,1,0:T(8,128)(2,1)S(1)} %all-to-all-done) | copy-start | bytes 6291460
  87.1 46.1 %all-to-all-start.2 = ((bf16[128,8,768]{0,2,1:T(8,128)(2,1)}), bf16[128,8,768]{0,2,1:T(8,128)(2,1)}, u32[]{:S(2)}, u32[]{:S(2)}) async-start(bf16[128,8,768]{0,2,1:T(8,128)(2,1)} %bitcast.87), calls=%async_computation.2 | async-start | bytes 3145728 | tf_op jit(solution)/shard_map/all_to_all | solution.py:36
  133.3 52.5 %all-to-all-start.1 = ((bf16[64,2,16,512]{3,2,1,0:T(8,128)(2,1)}), bf16[64,2,16,512]{3,2,1,0:T(8,128)(2,1)S(1)}, u32[]{:S(2)}, u32[]{:S(2)}) async-start(bf16[64,2,16,512]{3,2,1,0:T(8,128)(2,1)} %bitcast.85), calls=%async_computation.1 | async-start | bytes 4194304 | tf_op jit(solution)/shard_map/all_to_all | solution.py:55
  138.3 112.5 %all-gather.3.cloned.1.call-start = ((), (), s32[]{:S(2)}) async-start(), calls=%async_computation.4 | async-start | bytes 10485760 | tf_op jit(solution)/shard_map/all_gather | solution.py:54
  185.7 2.6 copy-start.1
  194.9 3.8 %copy-start.4 = (bf16[2,512,256]{2,1,0:T(8,128)(2,1)S(1)}, bf16[2,512,256]{2,1,0:T(8,128)(2,1)}, u32[]{:S(2)}) copy-start(bf16[2,512,256]{2,1,0:T(8,128)(2,1)} %custom-call) | copy-start | bytes 1572868
  203.4 2.3 copy-start
  206.9 1.9 copy-start.5
  208.7 1.4 copy-start.3
  217.1 2.2 copy-start
  220.5 1.9 copy-start.5
  222.4 1.4 copy-start.3
Sparse Core Ops, SparseCore 0:
  141.2 100.7 all-gather.2
